TPU v7x, 32 devices: a whole 2x2x4 slice. The times are simulated.
32 devices in a mesh: exp: 4 (over z), row: 4 (over y, core), col: 2 (over x).
Axes of the slice: x: 2, y: 2, z: 4, core: 2. Of those that a mesh axis runs over, the one named last changes fastest.
Arguments:
- exposures: float32 [64, 128, 1024], P('exp', 'row', 'col'), may hold values from -6 to 6
- bad_pixels: int32 [64, 128, 1024], P('exp', 'row', 'col'), may hold values 0 or 1
- offsets: int32 [64, 2], P('exp'), may hold values from -8 to 8, as said below
- warp_index: int32 [64, 2], P('exp'), may hold values from 0 to 15
- blur_index: int32 [64], P('exp'), may hold values from 0 to 7
Outputs:
- residual: float32 [64, 128, 1024], P('exp', 'row', 'col')
- median_sky: float32 [128, 1024], P('row', 'col')
Inputs may be any that keep to these rules, and one draw needn't show every extreme that they name: `offsets`: in each component some exposure has the offset -8 and some has 8.
All inputs are finite; a program needn't handle non-finite values. No bound on the sum of `bad_pixels` on one device may be relied on, other than what follows from the above.
Results may differ from a plain program's by a relative error of at most 0.0003.
Values sent between devices are 32-bit elements; how exact they have to be, the bound alone decides.
No kernel may reach another device: no remote copies, remote signals or barrier semaphores. Data moves between devices by JAX's collectives and lax.ppermute only.
A program may use at most 64 MiB of HBM per device.

v0:
```python
import jax
import jax.numpy as jnp
from jax import lax
from jax.sharding import PartitionSpec as P

NFRAC = 16
NPSF = 8
PSF_RADIUS = 4
PASSES = 16
HALO = 11
sentinel = 1000000.0
half_sentinel = 500000.0
pivot_span = 16.0


def _row_halo(block, dim, width):
    count = lax.axis_size("row")
    forward = [(i, i + 1) for i in range(count - 1)]
    backward = [(target, source) for source, target in forward]
    size = block.shape[dim]
    low = lax.ppermute(lax.slice_in_dim(block, size - width, None, axis=dim), "row", forward)
    high = lax.ppermute(lax.slice_in_dim(block, 0, width, axis=dim), "row", backward)
    return jnp.concatenate([low, block, high], axis=dim)


def _col_halo(block, dim, width):
    count = lax.axis_size("col")
    size = block.shape[dim]
    right_edge = lax.slice_in_dim(block, size - width, None, axis=dim)
    left_edge = lax.slice_in_dim(block, 0, width, axis=dim)
    if count != 2:
        forward = [(i, i + 1) for i in range(count - 1)]
        backward = [(target, source) for source, target in forward]
        low = lax.ppermute(right_edge, "col", forward)
        high = lax.ppermute(left_edge, "col", backward)
        return jnp.concatenate([low, block, high], axis=dim)
    first = lax.axis_index("col") == 0
    outgoing = jnp.moveaxis(jnp.where(first, right_edge, left_edge), dim, 0)
    packed_shape = outgoing.shape
    packed = outgoing.reshape(width, -1)
    arrived = lax.ppermute(packed, "col", [(0, 1), (1, 0)])
    arrived = jnp.moveaxis(arrived.reshape(packed_shape), 0, dim)
    zeros = jnp.zeros_like(arrived)
    low = jnp.where(first, zeros, arrived)
    high = jnp.where(first, arrived, zeros)
    return jnp.concatenate([low, block, high], axis=dim)


def extended(block, row_dim, col_dim, width):
    return _col_halo(_row_halo(block, row_dim, width), col_dim, width)


def lanczos_table():
    fraction = jnp.arange(NFRAC, dtype=jnp.float32) / NFRAC
    offset_grid = jnp.arange(-2, 4, dtype=jnp.float32)
    spread = offset_grid[None, :] - fraction[:, None]
    kernel = jnp.sinc(spread) * jnp.sinc(spread / 3.0)
    return kernel / jnp.sum(kernel, axis=1, keepdims=True)


def blur_table():
    offset_grid = jnp.arange(-PSF_RADIUS, PSF_RADIUS + 1, dtype=jnp.float32)
    widths = 0.7 + 0.2 * jnp.arange(NPSF, dtype=jnp.float32)
    kernel = jnp.exp(-0.5 * (offset_grid[None, :] / widths[:, None]) ** 2)
    return kernel / jnp.sum(kernel, axis=1, keepdims=True)


def lookup(indices, entries, kernel_table):
    chooser = (indices[:, None] == lax.broadcasted_iota(jnp.int32, (1, entries), 1)).astype(
        jnp.float32
    )
    return jnp.dot(chooser, kernel_table, precision=lax.Precision.HIGHEST)


def placed_taps(weights, shifts):
    reach = 2 * HALO + 1
    positions = lax.broadcasted_iota(jnp.int32, (1, 1, reach), 2)
    tap_slot = HALO + shifts[:, None, None] + lax.broadcasted_iota(jnp.int32, (1, 6, 1), 1) - 2
    spread = (tap_slot == positions).astype(jnp.float32)
    return jnp.sum(weights[:, :, None] * spread, axis=1)


def resample_axis(stack, coefficients, out_len, which_axis):
    out_shape = list(stack.shape)
    out_shape[which_axis] = out_len
    total = jnp.zeros(tuple(out_shape), jnp.float32)
    for position in range(2 * HALO + 1):
        window = lax.slice_in_dim(stack, position, position + out_len, 1, which_axis)
        total = total + coefficients[:, position, None, None] * window
    return total


def bisect_lower(valid_count, count_below):

    def one_pass(sweep_no, bounds):
        lower_edge, upper_edge = bounds
        middle = 0.5 * (lower_edge + upper_edge)
        enough = 2.0 * count_below(middle) >= valid_count
        return (jnp.where(enough, lower_edge, middle), jnp.where(enough, middle, upper_edge))

    initial = (
        jnp.full(valid_count.shape, -pivot_span, jnp.float32),
        jnp.full(valid_count.shape, pivot_span, jnp.float32),
    )
    return lax.fori_loop(0, PASSES, one_pass, initial)[0]


def stack_median(pixel_stack):
    valid_count = jnp.sum(pixel_stack < half_sentinel, axis=0, dtype=jnp.float32)

    def count_below(middle):
        return jnp.sum(pixel_stack <= middle[None], axis=0, dtype=jnp.float32)

    lower_edge = bisect_lower(valid_count, count_below)
    return jnp.min(jnp.where(pixel_stack > lower_edge[None], pixel_stack, sentinel), axis=0)


def body(exposures, bad_pixels, offsets, warp_index, blur_index):
    group_size, row_count, col_count = exposures.shape
    kernel_table = lanczos_table()
    coef_down = placed_taps(lookup(warp_index[:, 0], NFRAC, kernel_table), offsets[:, 0])
    coef_across = placed_taps(lookup(warp_index[:, 1], NFRAC, kernel_table), offsets[:, 1])
    padded = extended(exposures, 1, 2, HALO)
    across = resample_axis(padded, coef_down, row_count, 1)
    warped = resample_axis(across, coef_across, col_count, 2)
    flagged = jnp.where(bad_pixels == 1, sentinel, warped)
    band = stack_median(lax.all_to_all(flagged, "exp", split_axis=1, concat_axis=0, tiled=True))
    groups = lax.axis_size("exp")
    median_sky = lax.all_to_all(
        jnp.tile(band, (groups, 1)), "exp", split_axis=0, concat_axis=0, tiled=True
    )
    bordered = extended(median_sky, 0, 1, PSF_RADIUS)
    blur = blur_table()
    taps = 2 * PSF_RADIUS + 1
    blurred_rows = jnp.zeros((NPSF, row_count, col_count + 2 * PSF_RADIUS), jnp.float32)
    for tap_no in range(taps):
        blurred_rows = (
            blurred_rows
            + blur[:, tap_no, None, None] * bordered[None, tap_no : tap_no + row_count, :]
        )
    smoothed = jnp.zeros((NPSF, row_count, col_count), jnp.float32)
    for tap_no in range(taps):
        smoothed = (
            smoothed + blur[:, tap_no, None, None] * blurred_rows[:, :, tap_no : tap_no + col_count]
        )
    chooser = (blur_index[:, None] == lax.broadcasted_iota(jnp.int32, (1, NPSF), 1)).astype(
        jnp.float32
    )
    sky_model = jnp.zeros((group_size, row_count, col_count), jnp.float32)
    for kernel_no in range(NPSF):
        sky_model = sky_model + chooser[:, kernel_no, None, None] * smoothed[kernel_no][None]
    residual = jnp.where(bad_pixels == 1, 0.0, warped - sky_model)
    return (residual, median_sky)


def solution(mesh):
    return jax.shard_map(
        body,
        mesh=mesh,
        in_specs=(
            P("exp", "row", "col"),
            P("exp", "row", "col"),
            P("exp", None),
            P("exp", None),
            P("exp"),
        ),
        out_specs=(P("exp", "row", "col"), P("row", "col")),
        check_vma=False,
    )
```

profile of v0, /device:TPU:0, one launch (start us, length us, event | category | flops | bytes accessed | tf_op | source)
XLA Modules:
  0.0 90.9 jit_solution(72379477720639308)
XLA Ops:
  0.6 1.3 %fusion.134 = (f32[16,11,512]{2,1,0:T(8,128)S(1)}, f32[16,11,512]{2,1,0:T(8,128)S(1)}) fusion(f32[16,32,512]{2,1,0:T(8,128)} %param.8), kind=kLoop, calls=%fused_computation.315 | loop fusion | bytes 1441792 | tf_op jit(solution)/shard_map/slice | solution.py:22
  2.0 0.2 copy.47
  2.2 3.3 %collective-permute-start = (f32[16,11,512]{2,0,1:T(8,128)S(1)}, f32[16,11,512]{2,0,1:T(8,128)}, u32[]{:S(2)}, u32[]{:S(2)}) collective-permute-start(f32[16,11,512]{2,0,1:T(8,128)S(1)} %copy.47), channel_id=1, source_target_pairs={{0,2},{2,4},{4,6},{1,3},{3,5},{5,7},{8,10},{10,12},{12,14},{9,11},... | collective-permute-start | bytes 1081352 | tf_op jit(solution)/shard_map/ppermute | solution.py:21
  5.5 0.2 copy.48
  5.7 1.3 %collective-permute-start.1 = (f32[16,11,512]{2,0,1:T(8,128)S(1)}, f32[16,11,512]{2,0,1:T(8,128)S(1)}, u32[]{:S(2)}, u32[]{:S(2)}) collective-permute-start(f32[16,11,512]{2,0,1:T(8,128)S(1)} %copy.48), channel_id=1, source_target_pairs={{2,0},{4,2},{6,4},{3,1},{5,3},{7,5},{10,8},{12,10},{14,12},{11,9},... | collective-permute-start | bytes 1081352 | tf_op jit(solution)/shard_map/ppermute | solution.py:22
  7.2 0.2 fusion.67
  7.4 0.2 fusion.66
  7.7 0.8 slice_reduce_fusion.43
  8.5 1.1 %slice_reduce_fusion.44 = (f32[16]{0:T(128)}, f32[16]{0:T(128)}, f32[16]{0:T(128)}, f32[16]{0:T(128)}, f32[16]{0:T(128)}, /*index=5*/f32[16]{0:T(128)}, f32[16]{...) fusion(f32[16,23]{1,0:T(8,128)S(1)} %select_reduce_fusion), kind=kLoop, calls=%fused_computation.204 | loop fusion | bytes 2432 | tf_op jit(solution)/shard_map/slice | solution.py:89
  9.7 1.1 %slice_reduce_fusion.45 = (f32[16]{0:T(128)S(1)}, f32[16]{0:T(128)S(1)}, f32[16]{0:T(128)}, f32[16]{0:T(128)}, f32[16]{0:T(128)}, /*index=5*/f32[16]{0:T(128)}, ...) fusion(f32[16,23]{1,0:T(8,128)S(1)} %select_reduce_fusion.1), kind=kLoop, calls=%fused_computation.205 | loop fusion | bytes 2432 | tf_op jit(solution)/shard_map/slice | solution.py:89
  10.7 1.0 %constant_dynamic-update-slice_fusion.2 = f32[16,54,512]{2,0,1:T(8,128)S(1)} fusion(f32[16,11,512]{2,0,1:T(8,128)} %collective-permute-done), kind=kLoop, calls=%fused_computation.208 | loop fusion | bytes 720896
  11.8 0.6 constant_dynamic-update-slice_fusion.1
  12.4 0.2 fusion.53
  12.6 0.3 copy.40
  13.0 2.4 %collective-permute-start.2 = (f32[11,864]{1,0:T(8,128)S(1)}, f32[11,864]{1,0:T(8,128)S(1)}, u32[]{:S(2)}, u32[]{:S(2)}) collective-permute-start(f32[11,864]{1,0:T(8,128)S(1)} %reshape.187), channel_id=1, source_target_pairs={{0,1},{1,0},{2,3},{3,2},{4,5},{5,4},{6,7},{7,6},{8,9},{9,8},{10,11... | collective-permute-start | bytes 114056 | tf_op jit(solution)/shard_map/ppermute | solution.py:41
  15.4 0.2 slice_reduce_fusion.21
  15.6 1.9 %collective-permute-done.2 = f32[11,864]{1,0:T(8,128)S(1)} collective-permute-done((f32[11,864]{1,0:T(8,128)S(1)}, f32[11,864]{1,0:T(8,128)S(1)}, u32[]{:S(2)}, u32[]{:S(2)}) %collective-permute-start.2) | collective-permute-done | bytes 38048 | tf_op jit(solution)/shard_map/ppermute | solution.py:41
  17.6 0.3 copy.42
  18.1 0.3 copy.41
  18.6 0.7 pad_maximum_fusion
  19.8 3.9 %fusion = f32[16,32,534]{2,0,1:T(8,128)S(1)} fusion(f32[16,54,534]{2,0,1:T(8,128)S(1)} %pad_maximum_fusion, f32[16]{0:T(128)S(1)} %copy-done.24, f32[16]{0:T(128)S(1)} %copy-done.25, f32[16]{0:T(128)S(1)} %copy-done.26, f32[16]{0:T(128)S(1)} %copy-done.27, f32[16]{0:T(128)S(1)} %copy-done.28, f32[16]{0:T(128)S(1)} %copy-done.29, f32[16]{0:T(128)S(1)} %copy-done.30, ...), kind=kLoop, calls=%fused_computation.8 | loop fusion | flops 12303360 | bytes 26248640 | tf_op jit(solution)/shard_map/add | solution.py:89
  23.8 7.0 %broadcast_select_fusion = (f32[16,32,512]{2,0,1:T(8,128)}, f32[16,32,512]{2,0,1:T(8,128)S(1)}, pred[16,32,512]{2,0,1:T(8,128)(4,1)S(1)}) fusion(f32[16,32,534]{2,0,1:T(8,128)S(1)} %fusion, f32[16]{0:T(128)S(1)} %get-tuple-element.56, f32[16]{0:T(128)S(1)} %copy-done.2, f32[16]{0:T(128)S(1)} %copy-done.3, f32[16]{0:T(128)S(1)} %copy-done.4, ...), kind=kLoop, calls=%fused_computation.119 | loop fusion | flops 12320768 | bytes 27526592 | tf_op jit(solution)/shard_map/jit(_where)/select_n | solution.py:126
  30.8 5.4 %all-to-all-start = ((f32[16,32,512]{2,0,1:T(8,128)}), f32[16,32,512]{2,0,1:T(8,128)S(1)}, u32[]{:S(2)}, u32[]{:S(2)}) async-start(f32[16,32,512]{2,0,1:T(8,128)} %get-tuple-element.113), calls=%async_computation | async-start | bytes 2097152 | tf_op jit(solution)/shard_map/all_to_all | solution.py:127
  36.4 26.2 %all-to-all-done = f32[16,32,512]{2,0,1:T(8,128)S(1)} async-done(((f32[16,32,512]{2,0,1:T(8,128)}), f32[16,32,512]{2,0,1:T(8,128)S(1)}, u32[]{:S(2)}, u32[]{:S(2)}) %all-to-all-start) | async-done | bytes 1048608 | tf_op jit(solution)/shard_map/all_to_all | solution.py:127
  62.6 0.6 copy.43
  63.2 0.1 convert_reduce_fusion.1
  63.4 3.6 %while.13 = (s32[]{:T(128)}, f32[8,512]{1,0:T(8,128)S(1)}, f32[8,512]{1,0:T(8,128)S(1)}, f32[64,8,512]{2,1,0:T(8,128)S(1)}, f32[8,512]{1,0:T(8,128)S(1)}, /*index=5*/s32[]{:T(128)}, s32[]{:T(128)}) while((s32[]{:T(128)}, f32[8,512]{1,0:T(8,128)S(1)}, f32[8,512]{1,0:T(8,128)S(1)}, f32[64,8,512]{2,1,0:T(8,128)S(1)}, ...), condition=%wide.region_7.9_spmd.clone, body=%wide.region_5.8_spmd.clone.sunk | while | flops 1110019 | bytes 1302625 | solution.py:105
  63.4 0.1 convert_reduce_fusion.3
  63.6 0.1 convert_reduce_fusion.3
  63.9 0.1 convert_reduce_fusion.3
  64.1 0.1 convert_reduce_fusion.3
  64.3 0.1 convert_reduce_fusion.3
  64.5 0.1 convert_reduce_fusion.3
  64.8 0.1 convert_reduce_fusion.3
  67.0 0.2 fusion.22
  67.2 0.6 tile.2
  67.8 3.3 %all-to-all-start.1 = ((f32[4,8,512]{2,1,0:T(8,128)}), f32[4,8,512]{2,1,0:T(8,128)S(1)}, u32[]{:S(2)}, u32[]{:S(2)}) async-start(f32[4,8,512]{2,1,0:T(8,128)} %tile.2), calls=%async_computation.1 | async-start | bytes 131072 | tf_op jit(solution)/shard_map/all_to_all | solution.py:129
  71.1 5.8 %all-to-all-done.1 = f32[4,8,512]{2,1,0:T(8,128)S(1)} async-done(((f32[4,8,512]{2,1,0:T(8,128)}), f32[4,8,512]{2,1,0:T(8,128)S(1)}, u32[]{:S(2)}, u32[]{:S(2)}) %all-to-all-start.1) | async-done | bytes 65568 | tf_op jit(solution)/shard_map/all_to_all | solution.py:129
  76.9 1.3 %collective-permute-start.4 = (f32[4,512]{1,0:T(4,128)S(1)}, f32[4,512]{1,0:T(4,128)S(1)}, u32[]{:S(2)}, u32[]{:S(2)}) collective-permute-start(f32[4,512]{1,0:T(4,128)S(1)} %get-tuple-element.136), channel_id=1, source_target_pairs={{2,0},{4,2},{6,4},{3,1},{5,3},{7,5},{10,8},{12,10},{14,12},{11,9},... | collective-permute-start | bytes 24584 | tf_op jit(solution)/shard_map/ppermute | solution.py:22
  78.2 3.2 %collective-permute-start.3 = (f32[4,512]{1,0:T(4,128)S(1)}, f32[4,512]{1,0:T(4,128)S(1)}, u32[]{:S(2)}, u32[]{:S(2)}) collective-permute-start(f32[4,512]{1,0:T(4,128)S(1)} %get-tuple-element.135), channel_id=1, source_target_pairs={{0,2},{2,4},{4,6},{1,3},{3,5},{5,7},{8,10},{10,12},{12,14},{9,11},... | collective-permute-start | bytes 24584 | tf_op jit(solution)/shard_map/ppermute | solution.py:21
  81.5 0.6 collective-permute-done.3
  82.1 1.5 %collective-permute-start.5 = (f32[4,40]{0,1:T(8,128)S(1)}, f32[4,40]{0,1:T(8,128)S(1)}, u32[]{:S(2)}, u32[]{:S(2)}) collective-permute-start(f32[4,40]{0,1:T(8,128)S(1)} %fusion.55), channel_id=1, source_target_pairs={{0,1},{1,0},{2,3},{3,2},{4,5},{5,4},{6,7},{7,6},{8,9},{9,8},{10,11... | collective-permute-start | bytes 1928 | tf_op jit(solution)/shard_map/ppermute | solution.py:41
  83.7 2.3 %collective-permute-done.5 = f32[4,40]{0,1:T(8,128)S(1)} collective-permute-done((f32[4,40]{0,1:T(8,128)S(1)}, f32[4,40]{0,1:T(8,128)S(1)}, u32[]{:S(2)}, u32[]{:S(2)}) %collective-permute-start.5) | collective-permute-done | bytes 672 | tf_op jit(solution)/shard_map/ppermute | solution.py:41
  86.1 0.6 multiply_add_fusion
  86.7 1.3 %fusion.45 = f32[8,32,512]{2,1,0:T(8,128)S(1)} fusion(f32[8,32,520]{2,1,0:T(8,128)S(1)} %multiply_add_fusion, f32[8]{0:T(128)S(1)} %get-tuple-element.142, f32[8]{0:T(128)S(1)} %get-tuple-element.143, f32[8]{0:T(128)S(1)} %get-tuple-element.144, f32[8]{0:T(128)S(1)} %get-tuple-element.145, f32[8]{0:T(128)S(1)} %get-tuple-element.146, ...), kind=kLoop, calls=%fused_computation.103 | loop fusion | flops 2228224 | bytes 5243168 | tf_op jit(solution)/shard_map/add | solution.py:144
  88.0 0.7 subtract_select_fusion
  88.7 1.6 %copy.44 = f32[16,32,512]{2,1,0:T(8,128)} copy(f32[16,32,512]{2,0,1:T(8,128)S(1)} %subtract_select_fusion) | data formatting | bytes 2097152
  90.3 0.6 copy.62
  (192 shorter events, 3.3 us)
Async XLA Ops:
  2.0 5.1 %copy-start.41 = (s32[16,2]{0,1:T(2,128)S(1)}, s32[16,2]{0,1:T(2,128)}, u32[]{:S(2)}) copy-start(s32[16,2]{0,1:T(2,128)} %param.11) | copy-start | bytes 388
  2.0 5.1 %copy-start.42 = (s32[16,2]{0,1:T(2,128)S(1)}, s32[16,2]{0,1:T(2,128)}, u32[]{:S(2)}) copy-start(s32[16,2]{0,1:T(2,128)} %param.10) | copy-start | bytes 388
  2.2 9.6 %copy-start = (f32[16,32,512]{2,1,0:T(8,128)S(1)}, f32[16,32,512]{2,1,0:T(8,128)}, u32[]{:S(2)}) copy-start(f32[16,32,512]{2,1,0:T(8,128)} %param.8) | copy-start | bytes 3145732
  2.2 8.5 %collective-permute-start = (f32[16,11,512]{2,0,1:T(8,128)S(1)}, f32[16,11,512]{2,0,1:T(8,128)}, u32[]{:S(2)}, u32[]{:S(2)}) collective-permute-start(f32[16,11,512]{2,0,1:T(8,128)S(1)} %copy.47), channel_id=1, source_target_pairs={{0,2},{2,4},{4,6},{1,3},{3,5},{5,7},{8,10},{10,12},{12,14},{9,11},... | collective-permute-start | bytes 1081352 | tf_op jit(solution)/shard_map/ppermute | solution.py:21
  5.7 6.7 %collective-permute-start.1 = (f32[16,11,512]{2,0,1:T(8,128)S(1)}, f32[16,11,512]{2,0,1:T(8,128)S(1)}, u32[]{:S(2)}, u32[]{:S(2)}) collective-permute-start(f32[16,11,512]{2,0,1:T(8,128)S(1)} %copy.48), channel_id=1, source_target_pairs={{2,0},{4,2},{6,4},{3,1},{5,3},{7,5},{10,8},{12,10},{14,12},{11,9},... | collective-permute-start | bytes 1081352 | tf_op jit(solution)/shard_map/ppermute | solution.py:22
  13.0 4.5 %collective-permute-start.2 = (f32[11,864]{1,0:T(8,128)S(1)}, f32[11,864]{1,0:T(8,128)S(1)}, u32[]{:S(2)}, u32[]{:S(2)}) collective-permute-start(f32[11,864]{1,0:T(8,128)S(1)} %reshape.187), channel_id=1, source_target_pairs={{0,1},{1,0},{2,3},{3,2},{4,5},{5,4},{6,7},{7,6},{8,9},{9,8},{10,11... | collective-permute-start | bytes 114056 | tf_op jit(solution)/shard_map/ppermute | solution.py:41
  18.4 1.0 %copy-start.19 = (f32[16]{0:T(128)S(1)}, f32[16]{0:T(128)}, u32[]{:S(2)}) copy-start(f32[16]{0:T(128)} %get-tuple-element.97) | copy-start | bytes 196
  18.4 1.0 %copy-start.20 = (f32[16]{0:T(128)S(1)}, f32[16]{0:T(128)}, u32[]{:S(2)}) copy-start(f32[16]{0:T(128)} %get-tuple-element.98) | copy-start | bytes 196
  18.4 1.0 %copy-start.21 = (f32[16]{0:T(128)S(1)}, f32[16]{0:T(128)}, u32[]{:S(2)}) copy-start(f32[16]{0:T(128)} %get-tuple-element.99) | copy-start | bytes 196
  18.4 1.0 %copy-start.22 = (f32[16]{0:T(128)S(1)}, f32[16]{0:T(128)}, u32[]{:S(2)}) copy-start(f32[16]{0:T(128)} %get-tuple-element.100) | copy-start | bytes 196
  18.4 1.0 %copy-start.23 = (f32[16]{0:T(128)S(1)}, f32[16]{0:T(128)}, u32[]{:S(2)}) copy-start(f32[16]{0:T(128)} %get-tuple-element.78) | copy-start | bytes 196
  18.4 1.0 %copy-start.24 = (f32[16]{0:T(128)S(1)}, f32[16]{0:T(128)}, u32[]{:S(2)}) copy-start(f32[16]{0:T(128)} %get-tuple-element.79) | copy-start | bytes 196
  18.5 1.0 %copy-start.25 = (f32[16]{0:T(128)S(1)}, f32[16]{0:T(128)}, u32[]{:S(2)}) copy-start(f32[16]{0:T(128)} %get-tuple-element.80) | copy-start | bytes 196
  18.5 1.0 %copy-start.26 = (f32[16]{0:T(128)S(1)}, f32[16]{0:T(128)}, u32[]{:S(2)}) copy-start(f32[16]{0:T(128)} %get-tuple-element.81) | copy-start | bytes 196
  18.5 1.0 %copy-start.27 = (f32[16]{0:T(128)S(1)}, f32[16]{0:T(128)}, u32[]{:S(2)}) copy-start(f32[16]{0:T(128)} %get-tuple-element.82) | copy-start | bytes 196
  18.5 1.0 %copy-start.28 = (f32[16]{0:T(128)S(1)}, f32[16]{0:T(128)}, u32[]{:S(2)}) copy-start(f32[16]{0:T(128)} %get-tuple-element.83) | copy-start | bytes 196
  18.5 1.0 %copy-start.29 = (f32[16]{0:T(128)S(1)}, f32[16]{0:T(128)}, u32[]{:S(2)}) copy-start(f32[16]{0:T(128)} %get-tuple-element.84) | copy-start | bytes 196
  18.5 1.0 %copy-start.30 = (f32[16]{0:T(128)S(1)}, f32[16]{0:T(128)}, u32[]{:S(2)}) copy-start(f32[16]{0:T(128)} %get-tuple-element.85) | copy-start | bytes 196
  18.5 1.0 %copy-start.31 = (f32[16]{0:T(128)S(1)}, f32[16]{0:T(128)}, u32[]{:S(2)}) copy-start(f32[16]{0:T(128)} %get-tuple-element.86) | copy-start | bytes 196
  18.5 1.0 %copy-start.32 = (f32[16]{0:T(128)S(1)}, f32[16]{0:T(128)}, u32[]{:S(2)}) copy-start(f32[16]{0:T(128)} %get-tuple-element.87) | copy-start | bytes 196
  18.5 1.0 %copy-start.33 = (f32[16]{0:T(128)S(1)}, f32[16]{0:T(128)}, u32[]{:S(2)}) copy-start(f32[16]{0:T(128)} %get-tuple-element.88) | copy-start | bytes 196
  18.5 1.0 %copy-start.34 = (f32[16]{0:T(128)S(1)}, f32[16]{0:T(128)}, u32[]{:S(2)}) copy-start(f32[16]{0:T(128)} %get-tuple-element.89) | copy-start | bytes 196
  18.6 1.0 %copy-start.35 = (f32[16]{0:T(128)S(1)}, f32[16]{0:T(128)}, u32[]{:S(2)}) copy-start(f32[16]{0:T(128)} %get-tuple-element.90) | copy-start | bytes 196
  18.6 1.0 %copy-start.36 = (f32[16]{0:T(128)S(1)}, f32[16]{0:T(128)}, u32[]{:S(2)}) copy-start(f32[16]{0:T(128)} %get-tuple-element.91) | copy-start | bytes 196
  19.6 4.0 %copy-start.1 = (s32[16,32,512]{2,1,0:T(8,128)S(1)}, s32[16,32,512]{2,1,0:T(8,128)}, u32[]{:S(2)}) copy-start(s32[16,32,512]{2,1,0:T(8,128)} %param.9) | copy-start | bytes 3145732
  19.6 4.0 %copy-start.2 = (f32[16]{0:T(128)S(1)}, f32[16]{0:T(128)}, u32[]{:S(2)}) copy-start(f32[16]{0:T(128)} %get-tuple-element.57) | copy-start | bytes 196
  19.6 4.0 %copy-start.3 = (f32[16]{0:T(128)S(1)}, f32[16]{0:T(128)}, u32[]{:S(2)}) copy-start(f32[16]{0:T(128)} %get-tuple-element.58) | copy-start | bytes 196
  19.6 4.0 %copy-start.4 = (f32[16]{0:T(128)S(1)}, f32[16]{0:T(128)}, u32[]{:S(2)}) copy-start(f32[16]{0:T(128)} %get-tuple-element.59) | copy-start | bytes 196
  19.6 4.0 %copy-start.5 = (f32[16]{0:T(128)S(1)}, f32[16]{0:T(128)}, u32[]{:S(2)}) copy-start(f32[16]{0:T(128)} %get-tuple-element.60) | copy-start | bytes 196
  19.6 4.0 %copy-start.6 = (f32[16]{0:T(128)S(1)}, f32[16]{0:T(128)}, u32[]{:S(2)}) copy-start(f32[16]{0:T(128)} %get-tuple-element.61) | copy-start | bytes 196
  19.6 4.0 %copy-start.7 = (f32[16]{0:T(128)S(1)}, f32[16]{0:T(128)}, u32[]{:S(2)}) copy-start(f32[16]{0:T(128)} %get-tuple-element.62) | copy-start | bytes 196
  19.7 4.0 %copy-start.8 = (f32[16]{0:T(128)S(1)}, f32[16]{0:T(128)}, u32[]{:S(2)}) copy-start(f32[16]{0:T(128)} %get-tuple-element.63) | copy-start | bytes 196
  19.7 4.0 %copy-start.9 = (f32[16]{0:T(128)S(1)}, f32[16]{0:T(128)}, u32[]{:S(2)}) copy-start(f32[16]{0:T(128)} %get-tuple-element.64) | copy-start | bytes 196
  19.7 4.0 %copy-start.10 = (f32[16]{0:T(128)S(1)}, f32[16]{0:T(128)}, u32[]{:S(2)}) copy-start(f32[16]{0:T(128)} %get-tuple-element.65) | copy-start | bytes 196
  19.7 4.0 %copy-start.11 = (f32[16]{0:T(128)S(1)}, f32[16]{0:T(128)}, u32[]{:S(2)}) copy-start(f32[16]{0:T(128)} %get-tuple-element.66) | copy-start | bytes 196
  19.7 4.0 %copy-start.12 = (f32[16]{0:T(128)S(1)}, f32[16]{0:T(128)}, u32[]{:S(2)}) copy-start(f32[16]{0:T(128)} %get-tuple-element.67) | copy-start | bytes 196
  19.7 4.0 %copy-start.13 = (f32[16]{0:T(128)S(1)}, f32[16]{0:T(128)}, u32[]{:S(2)}) copy-start(f32[16]{0:T(128)} %get-tuple-element.68) | copy-start | bytes 196
  19.7 4.0 %copy-start.14 = (f32[16]{0:T(128)S(1)}, f32[16]{0:T(128)}, u32[]{:S(2)}) copy-start(f32[16]{0:T(128)} %get-tuple-element.69) | copy-start | bytes 196
  19.7 4.0 %copy-start.15 = (f32[16]{0:T(128)S(1)}, f32[16]{0:T(128)}, u32[]{:S(2)}) copy-start(f32[16]{0:T(128)} %get-tuple-element.70) | copy-start | bytes 196
  19.7 4.0 %copy-start.16 = (f32[16]{0:T(128)S(1)}, f32[16]{0:T(128)}, u32[]{:S(2)}) copy-start(f32[16]{0:T(128)} %get-tuple-element.71) | copy-start | bytes 196
  19.7 4.0 %copy-start.17 = (f32[16]{0:T(128)S(1)}, f32[16]{0:T(128)}, u32[]{:S(2)}) copy-start(f32[16]{0:T(128)} %get-tuple-element.72) | copy-start | bytes 196
  19.8 4.0 %copy-start.18 = (f32[16]{0:T(128)S(1)}, f32[16]{0:T(128)}, u32[]{:S(2)}) copy-start(f32[16]{0:T(128)} %get-tuple-element.73) | copy-start | bytes 196
  30.8 31.8 %all-to-all-start = ((f32[16,32,512]{2,0,1:T(8,128)}), f32[16,32,512]{2,0,1:T(8,128)S(1)}, u32[]{:S(2)}, u32[]{:S(2)}) async-start(f32[16,32,512]{2,0,1:T(8,128)} %get-tuple-element.113), calls=%async_computation | async-start | bytes 2097152 | tf_op jit(solution)/shard_map/all_to_all | solution.py:127
  67.0 14.4 %copy-start.43 = (s32[16]{0:T(128)S(1)}, s32[16]{0:T(128)}, u32[]{:S(2)}) copy-start(s32[16]{0:T(128)} %param.12) | copy-start | bytes 196
  67.8 9.1 %all-to-all-start.1 = ((f32[4,8,512]{2,1,0:T(8,128)}), f32[4,8,512]{2,1,0:T(8,128)S(1)}, u32[]{:S(2)}, u32[]{:S(2)}) async-start(f32[4,8,512]{2,1,0:T(8,128)} %tile.2), calls=%async_computation.1 | async-start | bytes 131072 | tf_op jit(solution)/shard_map/all_to_all | solution.py:129
  76.9 4.5 %collective-permute-start.4 = (f32[4,512]{1,0:T(4,128)S(1)}, f32[4,512]{1,0:T(4,128)S(1)}, u32[]{:S(2)}, u32[]{:S(2)}) collective-permute-start(f32[4,512]{1,0:T(4,128)S(1)} %get-tuple-element.136), channel_id=1, source_target_pairs={{2,0},{4,2},{6,4},{3,1},{5,3},{7,5},{10,8},{12,10},{14,12},{11,9},... | collective-permute-start | bytes 24584 | tf_op jit(solution)/shard_map/ppermute | solution.py:22
  78.2 3.8 %collective-permute-start.3 = (f32[4,512]{1,0:T(4,128)S(1)}, f32[4,512]{1,0:T(4,128)S(1)}, u32[]{:S(2)}, u32[]{:S(2)}) collective-permute-start(f32[4,512]{1,0:T(4,128)S(1)} %get-tuple-element.135), channel_id=1, source_target_pairs={{0,2},{2,4},{4,6},{1,3},{3,5},{5,7},{8,10},{10,12},{12,14},{9,11},... | collective-permute-start | bytes 24584 | tf_op jit(solution)/shard_map/ppermute | solution.py:21
  82.1 3.8 %collective-permute-start.5 = (f32[4,40]{0,1:T(8,128)S(1)}, f32[4,40]{0,1:T(8,128)S(1)}, u32[]{:S(2)}, u32[]{:S(2)}) collective-permute-start(f32[4,40]{0,1:T(8,128)S(1)} %fusion.55), channel_id=1, source_target_pairs={{0,1},{1,0},{2,3},{3,2},{4,5},{5,4},{6,7},{7,6},{8,9},{9,8},{10,11... | collective-permute-start | bytes 1928 | tf_op jit(solution)/shard_map/ppermute | solution.py:41
  (4 other events, 3.9 us)
where the time goes:
time: 91.4 us; the launch traced here: 90.9 us
  waiting for transfers between devices  36.9 us (40%)
  starting transfers between devices  21.6 us (24%)
  other arithmetic  18.2 us (20%)
  local copies, waits for them, and re-layouts  11.5 us (13%)
  between operations  1.6 us (2%)
    all_to_all x1, waiting for transfers between devices, body(): lax.all_to_all(flagged, 'exp', split_axis=1, concat_axis=0, tiled=True)  26.2 us
    select_n x1, other arithmetic, body(): flagged = jnp.where(bad_pixels == 1, sentinel, warped)  6.99 us
    ppermute x2, starting transfers between devices, _row_halo(): lax.ppermute(lax.slice_in_dim(block, size - width, None, axis=dim), 'row'...  6.48 us
    all_to_all x1, waiting for transfers between devices, body(): lax.all_to_all(jnp.tile(band, (groups, 1)), 'exp', split_axis=0, concat_a...  5.8 us
    all_to_all x1, starting transfers between devices, body(): lax.all_to_all(flagged, 'exp', split_axis=1, concat_axis=0, tiled=True)  5.4 us
    unnamed x94, local copies, waits for them, and re-layouts  4.46 us
    ppermute x2, waiting for transfers between devices, _col_halo(): arrived = lax.ppermute(packed, 'col', [(0, 1), (1, 0)])  4.23 us
    ppermute x2, starting transfers between devices, _col_halo(): arrived = lax.ppermute(packed, 'col', [(0, 1), (1, 0)])  3.87 us
  transfers between devices with their start and end apart: 8, of which 5 were waited for; matrix products, arithmetic and copies ran while one was open for 7% of the time, Pallas kernels for 0%

commit v1 on v0

--- a/solution.py
+++ b/solution.py
@@ -124,7 +124,15 @@
     across = resample_axis(padded, coef_down, row_count, 1)
     warped = resample_axis(across, coef_across, col_count, 2)
     flagged = jnp.where(bad_pixels == 1, sentinel, warped)
-    band = stack_median(lax.all_to_all(flagged, "exp", split_axis=1, concat_axis=0, tiled=True))
+
+    def plan_ratios(my_tile):
+        block_now = jax.lax.axis_size("exp")
+        z = jnp.split(my_tile, block_now, axis=1)
+        z_new = jnp.stack(z)
+        clean = jax.lax.all_to_all(z_new, axis_name="exp", split_axis=0, concat_axis=0)
+        return jnp.concatenate(clean, axis=0)
+
+    band = stack_median(plan_ratios(flagged))
     groups = lax.axis_size("exp")
     median_sky = lax.all_to_all(
         jnp.tile(band, (groups, 1)), "exp", split_axis=0, concat_axis=0, tiled=True

time: 91.4 us -> 88.3 us (0.966)
  local copies, waits for them, and re-layouts: 11.5 us -> 5.44 us
  other arithmetic: 18.2 us -> 21.5 us
    unnamed x94 -> x11, local copies, waits for them, and re-layouts: 4.46 us -> 0.65 us
    slice x4, local copies, waits for them, and re-layouts: 3.13 us -> 1.41 us  [resample_axis(): total = total + coefficients[:, position, None, None] * window]
    slice x1 -> x2, local copies, waits for them, and re-layouts: 0.01 us -> 1.4 us  [_row_halo(): lax.slice_in_dim(block, size - width, None, axis=dim)]
    slice x1 -> x0, local copies, waits for them, and re-layouts: 1.32 us -> none  [_row_halo(): lax.slice_in_dim(block, 0, width, axis=dim)]
    select_n x1, other arithmetic: 0.72 us -> 1.77 us  [body(): residual = jnp.where(bad_pixels == 1, 0.0, warped - sky_model)]
    another operation x0 -> x1, other arithmetic: none -> 1.04 us  [plan_ratios(): z_new = jnp.stack(z)]
  transfers between devices with their start and end apart: 8 -> 8, of which waited for: 5 -> 5; matrix products, arithmetic and copies ran while one was open for 7% -> 3% of each run, Pallas kernels for 0% -> 0%
where the time goes in v1:
time: 88.3 us; the launch traced here: 87.9 us
  waiting for transfers between devices  36.8 us (42%)
  starting transfers between devices  22.1 us (25%)
  other arithmetic  21.5 us (24%)
  local copies, waits for them, and re-layouts  5.44 us (6%)
  between operations  0.97 us (1%)
    all_to_all x1, waiting for transfers between devices, plan_ratios(): jax.lax.all_to_all(z_new, axis_name='exp', split_axis=0, concat_axis=0)  25.9 us
    select_n x1, other arithmetic, body(): flagged = jnp.where(bad_pixels == 1, sentinel, warped)  7.57 us
    ppermute x2, starting transfers between devices, _row_halo(): lax.ppermute(lax.slice_in_dim(block, size - width, None, axis=dim), 'row'...  6.27 us
    all_to_all x1, waiting for transfers between devices, body(): lax.all_to_all(jnp.tile(band, (groups, 1)), 'exp', split_axis=0, concat_a...  5.87 us
    all_to_all x1, starting transfers between devices, plan_ratios(): jax.lax.all_to_all(z_new, axis_name='exp', split_axis=0, concat_axis=0)  5.4 us
    ppermute x2, starting transfers between devices, _col_halo(): arrived = lax.ppermute(packed, 'col', [(0, 1), (1, 0)])  4.53 us
    ppermute x2, waiting for transfers between devices, _col_halo(): arrived = lax.ppermute(packed, 'col', [(0, 1), (1, 0)])  4.4 us
    add x1, other arithmetic, resample_axis(): total = total + coefficients[:, position, None, None] * window  4.15 us
  transfers between devices with their start and end apart: 8, of which 5 were waited for; matrix products, arithmetic and copies ran while one was open for 3% of the time, Pallas kernels for 0%

profile of v1, /device:TPU:0, one launch (start us, length us, event | category | flops | bytes accessed | tf_op | source)
XLA Modules:
  0.0 87.9 jit_solution(4788347216591767285)
XLA Ops:
  0.7 1.4 %fusion.135 = (f32[16,11,512]{2,1,0:T(8,128)S(1)}, f32[16,11,512]{2,1,0:T(8,128)S(1)}) fusion(f32[16,32,512]{2,1,0:T(8,128)} %param.8), kind=kLoop, calls=%fused_computation.319 | loop fusion | bytes 1441792 | tf_op jit(solution)/shard_map/slice | solution.py:21
  2.1 1.3 %collective-permute-start.1 = (f32[16,11,512]{2,1,0:T(8,128)S(1)}, f32[16,11,512]{2,1,0:T(8,128)S(1)}, u32[]{:S(2)}, u32[]{:S(2)}) collective-permute-start(f32[16,11,512]{2,1,0:T(8,128)S(1)} %get-tuple-element.115), channel_id=1, source_target_pairs={{2,0},{4,2},{6,4},{3,1},{5,3},{7,5},{10,8},{12,10},{14,12},{11,9},... | collective-permute-start | bytes 1081352 | tf_op jit(solution)/shard_map/ppermute | solution.py:22
  3.4 3.1 %collective-permute-start = (f32[16,11,512]{2,1,0:T(8,128)S(1)}, f32[16,11,512]{2,1,0:T(8,128)S(1)}, u32[]{:S(2)}, u32[]{:S(2)}) collective-permute-start(f32[16,11,512]{2,1,0:T(8,128)S(1)} %get-tuple-element.114), channel_id=1, source_target_pairs={{0,2},{2,4},{4,6},{1,3},{3,5},{5,7},{8,10},{10,12},{12,14},{9,11},... | collective-permute-start | bytes 1081352 | tf_op jit(solution)/shard_map/ppermute | solution.py:21
  6.6 0.2 fusion.68
  6.8 0.2 fusion.67
  7.2 0.2 slice_reduce_fusion.43
  7.4 0.5 slice_reduce_fusion.44
  8.0 0.5 slice_reduce_fusion.45
  8.5 0.2 fusion.54
  8.7 0.2 copy.17
  9.1 3.0 %collective-permute-start.2 = (f32[11,864]{1,0:T(8,128)S(1)}, f32[11,864]{1,0:T(8,128)S(1)}, u32[]{:S(2)}, u32[]{:S(2)}) collective-permute-start(f32[11,864]{1,0:T(8,128)S(1)} %reshape.190), channel_id=1, source_target_pairs={{0,1},{1,0},{2,3},{3,2},{4,5},{5,4},{6,7},{7,6},{8,9},{9,8},{10,11... | collective-permute-start | bytes 114056 | tf_op jit(solution)/shard_map/ppermute | solution.py:41
  12.1 0.2 slice_reduce_fusion.21
  12.3 1.9 %collective-permute-done.2 = f32[11,864]{1,0:T(8,128)S(1)} collective-permute-done((f32[11,864]{1,0:T(8,128)S(1)}, f32[11,864]{1,0:T(8,128)S(1)}, u32[]{:S(2)}, u32[]{:S(2)}) %collective-permute-start.2) | collective-permute-done | bytes 38048 | tf_op jit(solution)/shard_map/ppermute | solution.py:41
  14.4 0.3 copy.19
  14.8 0.3 copy.18
  15.0 1.0 %pad_maximum_fusion = f32[16,54,534]{2,1,0:T(8,128)S(1)} fusion(f32[16,54,11]{2,1,0:T(8,128)S(1)} %copy.19, f32[16,11,512]{2,1,0:T(8,128)S(1)} %collective-permute-done.1, f32[16,32,512]{2,1,0:T(8,128)S(1)} %copy-done, f32[16,11,512]{2,1,0:T(8,128)S(1)} %collective-permute-done, f32[16,54,11]{2,1,0:T(8,128)S(1)} %copy.18), kind=kLoop, calls=%fused_computation.6 | loop fusion | flops 1845504 | bytes 3691008 | tf_op jit(solution)/shard_map/concatenate | solution.py:46
  16.1 4.1 %fusion = f32[16,32,534]{2,1,0:T(8,128)S(1)} fusion(f32[16,54,534]{2,1,0:T(8,128)S(1)} %pad_maximum_fusion, f32[16]{0:T(128)S(1)} %get-tuple-element.73, f32[16]{0:T(128)S(1)} %get-tuple-element.74, f32[16]{0:T(128)S(1)} %get-tuple-element.75, f32[16]{0:T(128)S(1)} %get-tuple-element.76, f32[16]{0:T(128)S(1)} %get-tuple-element.77, ...), kind=kLoop, calls=%fused_computation.8 | loop fusion | flops 12303360 | bytes 26248640 | tf_op jit(solution)/shard_map/add | solution.py:89
  20.3 7.6 %broadcast_select_fusion = (f32[16,32,512]{2,1,0:T(8,128)S(1)}, f32[16,32,512]{2,1,0:T(8,128)S(1)}, pred[16,32,512]{2,1,0:T(8,128)(4,1)S(1)}) fusion(f32[16,32,534]{2,1,0:T(8,128)S(1)} %fusion, f32[16]{0:T(128)S(1)} %get-tuple-element.50, f32[16]{0:T(128)S(1)} %get-tuple-element.51, f32[16]{0:T(128)S(1)} %get-tuple-element.52, f32[16]{0:T(128)S(1)} %get-tuple-element.53, ...), kind=kLoop, calls=%fused_computation.119 | loop fusion | flops 12320768 | bytes 27526592 | tf_op jit(solution)/shard_map/jit(_where)/select_n | solution.py:126
  27.9 1.0 %pad_maximum_fusion.1 = f32[4,16,8,512]{3,2,1,0:T(8,128)} fusion(f32[1,16,8,512]{3,2,1,0:T(8,128)S(1)} %get-tuple-element.111, f32[1,16,8,512]{3,2,1,0:T(8,128)S(1)} %get-tuple-element.112, f32[1,16,8,512]{3,2,1,0:T(8,128)S(1)} %get-tuple-element.113, f32[1,16,8,512]{3,2,1,0:T(8,128)S(1)} %get-tuple-element.110), kind=kLoop, calls=%fused_computation.98 | loop fusion | flops 786432 | bytes 2097152 | tf_op jit(solution)/shard_map/stack | solution.py:131
  29.0 5.4 %all-to-all-start = ((f32[4,16,8,512]{3,2,1,0:T(8,128)}), f32[4,16,8,512]{3,2,1,0:T(8,128)S(1)}, u32[]{:S(2)}, u32[]{:S(2)}) async-start(f32[4,16,8,512]{3,2,1,0:T(8,128)} %pad_maximum_fusion.1), calls=%async_computation | async-start | bytes 2097152 | tf_op jit(solution)/shard_map/all_to_all | solution.py:132
  34.6 25.9 %all-to-all-done = f32[4,16,8,512]{3,2,1,0:T(8,128)S(1)} async-done(((f32[4,16,8,512]{3,2,1,0:T(8,128)}), f32[4,16,8,512]{3,2,1,0:T(8,128)S(1)}, u32[]{:S(2)}, u32[]{:S(2)}) %all-to-all-start) | async-done | bytes 1048608 | tf_op jit(solution)/shard_map/all_to_all | solution.py:132
  60.7 3.6 %while.13 = (s32[]{:T(128)}, f32[8,512]{1,0:T(8,128)S(1)}, f32[8,512]{1,0:T(8,128)S(1)}, f32[64,8,512]{2,1,0:T(8,128)S(1)}, f32[8,512]{1,0:T(8,128)S(1)}, /*index=5*/s32[]{:T(128)}, s32[]{:T(128)}) while((s32[]{:T(128)}, f32[8,512]{1,0:T(8,128)S(1)}, f32[8,512]{1,0:T(8,128)S(1)}, f32[64,8,512]{2,1,0:T(8,128)S(1)}, ...), condition=%wide.region_7.9_spmd.clone, body=%wide.region_5.8_spmd.clone.sunk | while | flops 1110019 | bytes 1302625 | solution.py:105
  60.7 0.1 convert_reduce_fusion.3
  60.9 0.1 convert_reduce_fusion.3
  61.1 0.1 convert_reduce_fusion.3
  61.4 0.1 convert_reduce_fusion.3
  61.6 0.1 convert_reduce_fusion.3
  61.8 0.1 convert_reduce_fusion.3
  62.0 0.1 convert_reduce_fusion.3
  62.3 0.1 convert_reduce_fusion.3
  62.5 0.1 convert_reduce_fusion.3
  62.7 0.1 convert_reduce_fusion.3
  63.2 0.1 convert_reduce_fusion.3
  63.6 0.1 convert_reduce_fusion.3
  64.1 0.1 convert_reduce_fusion.3
  64.3 0.2 fusion.22
  64.5 0.6 tile.2
  65.1 3.3 %all-to-all-start.1 = ((f32[4,8,512]{2,1,0:T(8,128)}), f32[4,8,512]{2,1,0:T(8,128)S(1)}, u32[]{:S(2)}, u32[]{:S(2)}) async-start(f32[4,8,512]{2,1,0:T(8,128)} %tile.2), calls=%async_computation.1 | async-start | bytes 131072 | tf_op jit(solution)/shard_map/all_to_all | solution.py:137
  68.4 5.9 %all-to-all-done.1 = f32[4,8,512]{2,1,0:T(8,128)S(1)} async-done(((f32[4,8,512]{2,1,0:T(8,128)}), f32[4,8,512]{2,1,0:T(8,128)S(1)}, u32[]{:S(2)}, u32[]{:S(2)}) %all-to-all-start.1) | async-done | bytes 65568 | tf_op jit(solution)/shard_map/all_to_all | solution.py:137
  74.3 1.3 %collective-permute-start.4 = (f32[4,512]{1,0:T(4,128)S(1)}, f32[4,512]{1,0:T(4,128)S(1)}, u32[]{:S(2)}, u32[]{:S(2)}) collective-permute-start(f32[4,512]{1,0:T(4,128)S(1)} %get-tuple-element.134), channel_id=1, source_target_pairs={{2,0},{4,2},{6,4},{3,1},{5,3},{7,5},{10,8},{12,10},{14,12},{11,9},... | collective-permute-start | bytes 24584 | tf_op jit(solution)/shard_map/ppermute | solution.py:22
  75.6 3.2 %collective-permute-start.3 = (f32[4,512]{1,0:T(4,128)S(1)}, f32[4,512]{1,0:T(4,128)S(1)}, u32[]{:S(2)}, u32[]{:S(2)}) collective-permute-start(f32[4,512]{1,0:T(4,128)S(1)} %get-tuple-element.133), channel_id=1, source_target_pairs={{0,2},{2,4},{4,6},{1,3},{3,5},{5,7},{8,10},{10,12},{12,14},{9,11},... | collective-permute-start | bytes 24584 | tf_op jit(solution)/shard_map/ppermute | solution.py:21
  78.8 0.6 collective-permute-done.3
  79.5 1.5 %collective-permute-start.5 = (f32[4,40]{0,1:T(8,128)S(1)}, f32[4,40]{0,1:T(8,128)S(1)}, u32[]{:S(2)}, u32[]{:S(2)}) collective-permute-start(f32[4,40]{0,1:T(8,128)S(1)} %fusion.56), channel_id=1, source_target_pairs={{0,1},{1,0},{2,3},{3,2},{4,5},{5,4},{6,7},{7,6},{8,9},{9,8},{10,11... | collective-permute-start | bytes 1928 | tf_op jit(solution)/shard_map/ppermute | solution.py:41
  81.0 2.5 %collective-permute-done.5 = f32[4,40]{0,1:T(8,128)S(1)} collective-permute-done((f32[4,40]{0,1:T(8,128)S(1)}, f32[4,40]{0,1:T(8,128)S(1)}, u32[]{:S(2)}, u32[]{:S(2)}) %collective-permute-start.5) | collective-permute-done | bytes 672 | tf_op jit(solution)/shard_map/ppermute | solution.py:41
  83.6 0.6 multiply_add_fusion
  84.2 1.3 %fusion.45 = f32[8,32,512]{2,1,0:T(8,128)S(1)} fusion(f32[8,32,520]{2,1,0:T(8,128)S(1)} %multiply_add_fusion, f32[8]{0:T(128)S(1)} %get-tuple-element.140, f32[8]{0:T(128)S(1)} %get-tuple-element.141, f32[8]{0:T(128)S(1)} %get-tuple-element.142, f32[8]{0:T(128)S(1)} %get-tuple-element.143, f32[8]{0:T(128)S(1)} %get-tuple-element.144, ...), kind=kLoop, calls=%fused_computation.103 | loop fusion | flops 2228224 | bytes 5243168 | tf_op jit(solution)/shard_map/add | solution.py:152
  85.5 1.8 %subtract_select_fusion = f32[16,32,512]{2,1,0:T(8,128)} fusion(pred[16,32,512]{2,1,0:T(8,128)(4,1)S(1)} %get-tuple-element.109, f32[16,32,512]{2,1,0:T(8,128)S(1)} %get-tuple-element.108, f32[32,512]{1,0:T(8,128)S(1)} %get-tuple-element.117, f32[16]{0:T(128)S(1)} %get-tuple-element.149, f32[32,512]{1,0:T(8,128)S(1)} %get-tuple-element.118, ...), kind=kLoop, calls=%fused_computation.99 | loop fusion | flops 4456448 | bytes 2884096 | tf_op jit(solution)/shard_map/jit(_where)/select_n | solution.py:160
  87.3 0.6 copy.30
  (109 shorter events, 2.4 us)
Async XLA Ops:
  0.6 7.9 %copy-start = (f32[16,32,512]{2,1,0:T(8,128)S(1)}, f32[16,32,512]{2,1,0:T(8,128)}, u32[]{:S(2)}) copy-start(f32[16,32,512]{2,1,0:T(8,128)} %param.8) | copy-start | bytes 3145732
  0.6 5.8 %copy-start.2 = (s32[16,2]{0,1:T(2,128)S(1)}, s32[16,2]{0,1:T(2,128)}, u32[]{:S(2)}) copy-start(s32[16,2]{0,1:T(2,128)} %param.11) | copy-start | bytes 388
  0.6 5.8 %copy-start.3 = (s32[16,2]{0,1:T(2,128)S(1)}, s32[16,2]{0,1:T(2,128)}, u32[]{:S(2)}) copy-start(s32[16,2]{0,1:T(2,128)} %param.10) | copy-start | bytes 388
  2.1 6.4 %collective-permute-start.1 = (f32[16,11,512]{2,1,0:T(8,128)S(1)}, f32[16,11,512]{2,1,0:T(8,128)S(1)}, u32[]{:S(2)}, u32[]{:S(2)}) collective-permute-start(f32[16,11,512]{2,1,0:T(8,128)S(1)} %get-tuple-element.115), channel_id=1, source_target_pairs={{2,0},{4,2},{6,4},{3,1},{5,3},{7,5},{10,8},{12,10},{14,12},{11,9},... | collective-permute-start | bytes 1081352 | tf_op jit(solution)/shard_map/ppermute | solution.py:22
  3.4 5.1 %collective-permute-start = (f32[16,11,512]{2,1,0:T(8,128)S(1)}, f32[16,11,512]{2,1,0:T(8,128)S(1)}, u32[]{:S(2)}, u32[]{:S(2)}) collective-permute-start(f32[16,11,512]{2,1,0:T(8,128)S(1)} %get-tuple-element.114), channel_id=1, source_target_pairs={{0,2},{2,4},{4,6},{1,3},{3,5},{5,7},{8,10},{10,12},{12,14},{9,11},... | collective-permute-start | bytes 1081352 | tf_op jit(solution)/shard_map/ppermute | solution.py:21
  9.1 5.2 %collective-permute-start.2 = (f32[11,864]{1,0:T(8,128)S(1)}, f32[11,864]{1,0:T(8,128)S(1)}, u32[]{:S(2)}, u32[]{:S(2)}) collective-permute-start(f32[11,864]{1,0:T(8,128)S(1)} %reshape.190), channel_id=1, source_target_pairs={{0,1},{1,0},{2,3},{3,2},{4,5},{5,4},{6,7},{7,6},{8,9},{9,8},{10,11... | collective-permute-start | bytes 114056 | tf_op jit(solution)/shard_map/ppermute | solution.py:41
  16.1 4.2 %copy-start.1 = (s32[16,32,512]{2,1,0:T(8,128)S(1)}, s32[16,32,512]{2,1,0:T(8,128)}, u32[]{:S(2)}) copy-start(s32[16,32,512]{2,1,0:T(8,128)} %param.9) | copy-start | bytes 3145732
  29.0 31.5 %all-to-all-start = ((f32[4,16,8,512]{3,2,1,0:T(8,128)}), f32[4,16,8,512]{3,2,1,0:T(8,128)S(1)}, u32[]{:S(2)}, u32[]{:S(2)}) async-start(f32[4,16,8,512]{3,2,1,0:T(8,128)} %pad_maximum_fusion.1), calls=%async_computation | async-start | bytes 2097152 | tf_op jit(solution)/shard_map/all_to_all | solution.py:132
  64.3 14.5 %copy-start.4 = (s32[16]{0:T(128)S(1)}, s32[16]{0:T(128)}, u32[]{:S(2)}) copy-start(s32[16]{0:T(128)} %param.12) | copy-start | bytes 196
  65.1 9.2 %all-to-all-start.1 = ((f32[4,8,512]{2,1,0:T(8,128)}), f32[4,8,512]{2,1,0:T(8,128)S(1)}, u32[]{:S(2)}, u32[]{:S(2)}) async-start(f32[4,8,512]{2,1,0:T(8,128)} %tile.2), calls=%async_computation.1 | async-start | bytes 131072 | tf_op jit(solution)/shard_map/all_to_all | solution.py:137
  74.3 4.5 %collective-permute-start.4 = (f32[4,512]{1,0:T(4,128)S(1)}, f32[4,512]{1,0:T(4,128)S(1)}, u32[]{:S(2)}, u32[]{:S(2)}) collective-permute-start(f32[4,512]{1,0:T(4,128)S(1)} %get-tuple-element.134), channel_id=1, source_target_pairs={{2,0},{4,2},{6,4},{3,1},{5,3},{7,5},{10,8},{12,10},{14,12},{11,9},... | collective-permute-start | bytes 24584 | tf_op jit(solution)/shard_map/ppermute | solution.py:22
  75.6 3.8 %collective-permute-start.3 = (f32[4,512]{1,0:T(4,128)S(1)}, f32[4,512]{1,0:T(4,128)S(1)}, u32[]{:S(2)}, u32[]{:S(2)}) collective-permute-start(f32[4,512]{1,0:T(4,128)S(1)} %get-tuple-element.133), channel_id=1, source_target_pairs={{0,2},{2,4},{4,6},{1,3},{3,5},{5,7},{8,10},{10,12},{12,14},{9,11},... | collective-permute-start | bytes 24584 | tf_op jit(solution)/shard_map/ppermute | solution.py:21
  79.5 4.0 %collective-permute-start.5 = (f32[4,40]{0,1:T(8,128)S(1)}, f32[4,40]{0,1:T(8,128)S(1)}, u32[]{:S(2)}, u32[]{:S(2)}) collective-permute-start(f32[4,40]{0,1:T(8,128)S(1)} %fusion.56), channel_id=1, source_target_pairs={{0,1},{1,0},{2,3},{3,2},{4,5},{5,4},{6,7},{7,6},{8,9},{9,8},{10,11... | collective-permute-start | bytes 1928 | tf_op jit(solution)/shard_map/ppermute | solution.py:41
